TPU v7x, 512 devices: a whole 4x8x8 slice. The times are simulated.
512 devices in a mesh: req: 4 (over x), exp: 8 (over z), shard: 16 (over y, core).
Axes of the slice: x: 4, y: 8, z: 8, core: 2. Of those that a mesh axis runs over, the one named last changes fastest.
Arguments:
- query_stretch: bfloat16 [8, 128, 2304], P('req', 'exp'), may hold values from -8 to 8
- resid_stretch: bfloat16 [8, 128, 2304], P('req', 'exp'), may hold values from -30 to 30
- route_ids: int32 [8, 128, 2], P('req', 'exp'), may hold values from 0 to 7, all different within a row; in each aligned block of 16 rows (0 to 15, 16 to 31, ..., all dimensions but the last counted through in order) at most 6 rows name the same one
- route_probs: bfloat16 [8, 128, 2], P('req', 'exp'), may hold values from 0.19921875 to 1
- request_order: int32 [8], replicated, may hold values from 0 to 7, each once
- prior_pages: int32 [4, 2], P('req'), may hold values from 63 to 189, as said below
- page_order: int32 [4, 256], P('req'), may hold values from 0 to 255, each once within a row
- key_pool: bfloat16 [4, 256, 64, 2304], P('req', ('exp', 'shard')), may hold values from -8 to 8
- value_pool: bfloat16 [4, 256, 64, 2304], P('req', ('exp', 'shard')), may hold values from -6 to 6
- norm_gain: float32 [2304], replicated, may hold values from 0.4 to 2.5
- out_proj: bfloat16 [2304, 2304], P('shard'), may hold values from -0.125 to 0.125
- gate_up: bfloat16 [8, 2, 2880, 2304], P('exp', None, 'shard'), may hold values from -0.125 to 0.125
- down_proj: bfloat16 [8, 2880, 2304], P('exp', 'shard'), may hold values from -0.109375 to 0.109375
Outputs:
- mixed_out: bfloat16 [8, 128, 2304], P('req', 'exp')
Inputs may be any that keep to these rules, and one draw needn't show every extreme that they name: `route_ids`: each row names 2 different experts. In each aligned block of 16 rows (one request's tokens b * 16 to (b + 1) * 16 - 1) no expert is named by more than 6 rows, a bound that some block reaches. `request_order`: A permutation of the requests. `prior_pages`: in each group the 2 counts sum to 252, so that the pool is full; one member of every group has exactly 189. `page_order`: each row is a permutation of the group's pool pages.
All inputs are finite; a program needn't handle non-finite values.
Results may differ from a plain program's by a relative error of at most 0.02.
Values may be sent and summed in bfloat16 or wider, within the bound.
No kernel may reach another device: no remote copies, remote signals or barrier semaphores. Data moves between devices by JAX's collectives and lax.ppermute only.
A program may use at most 64 MiB of HBM per device.

v0:
```python
import math
import jax
import jax.numpy as jnp
from jax import lax
from jax.sharding import PartitionSpec as P

H = 36
NEG_FILL = -1e30
EPSILON = 1e-06


def expert_rows(received, gate_up, down_proj):
    width = received.shape[-1]
    flat_rows = received.reshape(-1, width)
    both = lax.dot_general(
        flat_rows, gate_up[0], (((1,), (2,)), ((), ())), preferred_element_type=jnp.float32
    )
    active = (jax.nn.silu(both[:, 0]) * both[:, 1]).astype(jnp.bfloat16)
    partial_out = jnp.dot(active, down_proj[0], preferred_element_type=jnp.float32)
    return partial_out.reshape(received.shape)


def on_device(
    query_stretch,
    resid_stretch,
    route_ids,
    route_probs,
    request_order,
    prior_pages,
    page_order,
    key_pool,
    value_pool,
    norm_gain,
    out_proj,
    gate_up,
    down_proj,
):
    members = prior_pages.shape[1]
    tokens_here = query_stretch.shape[1]
    width = query_stretch.shape[2]
    head_size = width // H
    group_index = lax.axis_index("req")
    exp_index = lax.axis_index("exp")
    shard_index = lax.axis_index("shard")
    shard_count = lax.axis_size("shard")
    experts_count = lax.axis_size("exp")
    all_query, all_resid, all_ids, all_probs = (
        lax.all_gather(query_stretch, "req", axis=0, tiled=True),
        lax.all_gather(resid_stretch, "req", axis=0, tiled=True),
        lax.all_gather(route_ids, "req", axis=0, tiled=True),
        lax.all_gather(route_probs, "req", axis=0, tiled=True),
    )
    served = lax.dynamic_slice_in_dim(request_order, group_index * members, members)
    served_query = jnp.take(all_query, served, axis=0)
    served_resid = jnp.take(all_resid, served, axis=0)
    served_ids = jnp.take(all_ids, served, axis=0)
    served_probs = jnp.take(all_probs, served, axis=0)
    group_query = lax.all_gather(served_query, "exp", axis=1, tiled=True)
    stretch_len = group_query.shape[1]
    pages_here = key_pool.shape[1]
    page_size = key_pool.shape[2]
    device_index = exp_index * shard_count + shard_index
    physical = device_index * pages_here + jnp.arange(pages_here, dtype=jnp.int32)
    page_row = page_order[0]
    pool_size = page_row.shape[0]
    matched = page_row[None, :] == physical[:, None]
    located = jnp.sum(
        jnp.where(matched, jnp.arange(pool_size, dtype=jnp.int32)[None, :], 0), axis=1
    )
    prior_row = prior_pages[0]
    page_counts = prior_row + stretch_len // page_size
    page_ends = jnp.cumsum(page_counts)
    page_starts = page_ends - page_counts
    owner_slot = jnp.sum((located[:, None] >= page_ends[None, :]).astype(jnp.int32), axis=1)
    owner_hot = owner_slot[:, None] == jnp.arange(members, dtype=jnp.int32)[None, :]
    logical = located - jnp.sum(jnp.where(owner_hot, page_starts[None, :], 0), axis=1)
    prior_here = jnp.sum(jnp.where(owner_hot, prior_row[None, :], 0), axis=1)
    key_place = logical[:, None] * page_size + jnp.arange(page_size, dtype=jnp.int32)[None, :]
    query_place = (
        prior_here[:, None] * page_size + jnp.arange(stretch_len, dtype=jnp.int32)[None, :]
    )
    visible = key_place[:, None, :] <= query_place[:, :, None]
    page_query = jnp.take(group_query, owner_slot, axis=0).reshape(
        pages_here, stretch_len, H, head_size
    )
    key_rows = key_pool[0].reshape(pages_here, page_size, H, head_size)
    value_rows = value_pool[0].reshape(pages_here, page_size, H, head_size)
    scores = jnp.einsum(
        "pqhd,pkhd->phqk", page_query, key_rows, preferred_element_type=jnp.float32
    ) * (1.0 / math.sqrt(head_size))
    scores = jnp.where(visible[:, None, :, :], scores, NEG_FILL)
    page_peak = jnp.max(scores, axis=3)
    local_peak = jnp.max(
        jnp.where(owner_hot[:, :, None, None], page_peak[:, None], NEG_FILL), axis=0
    )
    row_peak = lax.pmax(local_peak, ("exp", "shard"))
    peak_here = jnp.take(row_peak, owner_slot, axis=0)
    weights_bf = jnp.where(
        visible[:, None, :, :], jnp.exp(scores - peak_here[..., None]), 0.0
    ).astype(jnp.bfloat16)
    page_totals = jnp.sum(weights_bf, axis=3, dtype=jnp.float32)
    page_context = jnp.einsum(
        "phqk,pkhd->pqhd", weights_bf, value_rows, preferred_element_type=jnp.float32
    )
    page_context = page_context.reshape(pages_here, stretch_len, width)
    context = jnp.sum(jnp.where(owner_hot[:, :, None, None], page_context[:, None], 0.0), axis=0)
    totals = jnp.sum(jnp.where(owner_hot[:, :, None, None], page_totals[:, None], 0.0), axis=0)
    context_all, totals_all = lax.psum((context, totals), ("exp", "shard"))
    context_mine = lax.dynamic_slice_in_dim(context_all, exp_index * tokens_here, tokens_here, 1)
    totals_mine = lax.dynamic_slice_in_dim(totals_all, exp_index * tokens_here, tokens_here, 2)
    per_head = context_mine.reshape(members, tokens_here, H, head_size)
    attended = (
        (per_head / jnp.transpose(totals_mine, (0, 2, 1))[..., None])
        .reshape(members, tokens_here, width)
        .astype(jnp.bfloat16)
    )
    projected_part = lax.dot_general(
        attended, out_proj, (((2,), (1,)), ((), ())), preferred_element_type=jnp.float32
    ).astype(jnp.bfloat16)
    projected = lax.all_gather(projected_part, "shard", axis=2, tiled=True)
    hidden_state = served_resid.astype(jnp.float32) + projected.astype(jnp.float32)
    mean_square = jnp.mean(hidden_state * hidden_state, axis=2, keepdims=True)
    normed = (hidden_state * lax.rsqrt(mean_square + EPSILON) * norm_gain).astype(jnp.bfloat16)
    top_count = served_ids.shape[2]
    capacity = min(tokens_here, max(2, 3 * tokens_here * top_count // (2 * experts_count)))
    flat_ids = served_ids.reshape(members, tokens_here * top_count)
    expert_hot = (
        flat_ids[:, :, None] == jnp.arange(experts_count, dtype=jnp.int32)[None, None, :]
    ).astype(jnp.int32)
    before = jnp.cumsum(expert_hot, axis=1) - expert_hot
    slot_place = jnp.sum(before * expert_hot, axis=2)
    slot_hot = (
        slot_place[:, :, None] == jnp.arange(capacity, dtype=jnp.int32)[None, None, :]
    ).astype(jnp.int32)
    place_table = (expert_hot[:, :, :, None] * slot_hot[:, :, None, :]).reshape(
        members, tokens_here, top_count, experts_count, capacity
    )
    pick_table = jnp.sum(place_table, axis=2).astype(jnp.bfloat16)
    sent_rows = jnp.einsum(
        "jtnc,jtd->njcd", pick_table, normed, preferred_element_type=jnp.float32
    ).astype(jnp.bfloat16)
    share_table = jnp.sum(
        place_table.astype(jnp.bfloat16) * served_probs[:, :, :, None, None], axis=2
    )
    partial_out = expert_rows(
        lax.all_to_all(sent_rows, "exp", split_axis=0, concat_axis=0, tiled=True),
        gate_up,
        down_proj,
    )
    expert_out = lax.psum(partial_out.astype(jnp.bfloat16), "shard")
    returned = lax.all_to_all(expert_out, "exp", split_axis=0, concat_axis=0, tiled=True)
    moe_term = jnp.einsum(
        "jtnc,njcd->jtd", share_table, returned, preferred_element_type=jnp.float32
    )
    mixed_out = (hidden_state + moe_term).astype(jnp.bfloat16)
    return mixed_out


def solution(mesh):
    return jax.shard_map(
        on_device,
        mesh=mesh,
        in_specs=(
            P("req", "exp", None),
            P("req", "exp", None),
            P("req", "exp", None),
            P("req", "exp", None),
            P(),
            P("req", None),
            P("req", None),
            P("req", ("exp", "shard"), None, None),
            P("req", ("exp", "shard"), None, None),
            P(),
            P("shard", None),
            P("exp", None, "shard", None),
            P("exp", "shard", None),
        ),
        out_specs=P("req", "exp", None),
        check_vma=False,
    )
```

profile of v0, /device:TPU:1, one launch (start us, length us, event | category | flops | bytes accessed | tf_op | source)
XLA Modules:
  0.0 1259.9 jit_solution(11993732823770950947)
XLA Ops:
  6.5 0.9 compare_and_fusion
  7.4 11.4 all_gather.19
  18.9 0.6 gather_fusion.5
  19.4 0.7 broadcast_select_fusion
  20.2 8.2 all_gather.22
  28.5 0.6 gather_fusion.2
  29.4 0.7 add_bitcast_fusion
  30.2 0.7 fusion.29
  30.9 0.9 fusion.26
  31.7 0.2 fusion.27
  31.9 0.6 reduce_window_sum.18
  32.6 2.8 reshape_squeeze.6
  35.4 1.4 copy.110
  36.8 0.2 select_reduce_fusion.5
  36.9 10.4 all_gather.18
  47.8 18.5 %all-gather.2.cloned.1.call-done = bf16[2,128,2304]{2,1,0:T(8,128)(2,1)} async-done(((bf16[2,16,2304]{2,1,0:T(8,128)(2,1)}), bf16[2,128,2304]{2,1,0:T(8,128)(2,1)}) %all-gather.2.cloned.1.call-update) | async-done | bytes 1179664 | tf_op jit(solution)/shard_map/all_gather | solution.py:58
  66.3 1.9 gather_fusion
  68.2 1.4 copy.90
  69.6 3.8 fusion.3
  73.6 490.0 %pmax.7 = f32[2,36,128]{2,1,0:T(8,128)S(1)} all-reduce(f32[2,36,128]{2,1,0:T(8,128)S(1)} %copy.92), channel_id=1, replica_groups=mesh['req'=4,'exp'=8,'shard'=16] {'exp','shard'}, use_global_device_ids=true, to_apply=%region_7.9 | all-reduce | flops 9216 | bytes 73728 | tf_op jit(solution)/shard_map/pmax | solution.py:96
  563.6 0.5 gather_fusion.1
  564.2 3.7 fusion.32
  567.9 3.1 copy.94
  571.0 3.7 select_reduce_fusion
  574.8 0.7 copy-done.5
  575.5 0.2 select_reduce_fusion.3
  575.8 0.6 gather_fusion.4
  576.4 2.4 convert_reduce_fusion
  578.9 491.2 %psum.22 = f32[2,36,128]{2,0,1:T(2,128)S(1)} all-reduce(f32[2,36,128]{2,0,1:T(2,128)S(1)} %select_reduce_fusion.1), channel_id=1, replica_groups=mesh['req'=4,'exp'=8,'shard'=16] {'exp','shard'}, use_global_device_ids=true, to_apply=%region_12.14 | all-reduce | flops 9216 | bytes 73728 | tf_op jit(solution)/shard_map/psum | solution.py:108
  1070.3 0.2 div.23
  1070.5 0.2 div.24
  1070.8 1.5 convolution_convert_fusion.2
  1072.4 23.8 %all_gather.21 = bf16[2,16,2304]{1,0,2:T(2,128)(2,1)S(1)} all-gather(bf16[2,16,144]{1,0,2:T(2,128)(2,1)S(1)} %copy.96), channel_id=1, replica_groups=mesh['req'=4,'exp'=8,'shard'=16] {'shard'}, dimensions={2}, use_global_device_ids=true | all-gather | bytes 156672 | tf_op jit(solution)/shard_map/all_gather | solution.py:120
  1096.3 1.4 copy.97
  1097.7 0.2 multiply_reduce_fusion
  1097.9 0.3 fusion
  1098.2 0.3 copy.100
  1098.6 20.1 %all_to_all.10 = bf16[8,2,6,2304]{3,1,2,0:T(2,128)(2,1)S(1)} all-to-all(bf16[8,2,6,2304]{3,1,2,0:T(2,128)(2,1)S(1)} %copy.100), channel_id=1, replica_groups=mesh['req'=4,'exp'=8,'shard'=16] {'exp'}, dimensions={0} | all-to-all | bytes 884736 | tf_op jit(solution)/shard_map/all_to_all | solution.py:146
  1118.7 0.9 reshape.247
  1119.6 1.6 fusion.4
  1121.5 1.0 convolution_convert_fusion.1
  1122.5 105.0 %all-reduce.5.cloned.1.call-done = bf16[8,2,6,2304]{3,0,2,1:T(8,128)(2,1)} async-done(((bf16[8,2,6,2304]{3,0,2,1:T(8,128)(2,1)}), bf16[8,2,6,2304]{3,0,2,1:T(8,128)(2,1)}) %all-reduce.5.cloned.1.call-update) | async-done | bytes 442384 | tf_op jit(solution)/shard_map/psum | solution.py:150
  1227.5 2.1 copy.105
  1229.6 6.7 all-to-all-start.1
  1236.3 7.9 all_gather.23
  1244.2 0.6 gather_fusion.3
  1244.9 7.6 all-to-all-done.1
  1252.5 0.9 fusion.2
  (59 shorter events, 2.3 us)
Async XLA Ops:
  6.5 1113.1 %copy-start = (bf16[1,2,180,2304]{3,1,2,0:T(2,128)(2,1)S(1)}, bf16[1,2,180,2304]{3,1,2,0:T(2,128)(2,1)}, u32[]{:S(2)}) copy-start(bf16[1,2,180,2304]{3,1,2,0:T(2,128)(2,1)} %param.26) | copy-start | bytes 4976644
  6.5 28.8 %copy-start.3 = (bf16[1,2,64,2304]{3,2,1,0:T(8,128)(2,1)S(1)}, bf16[1,2,64,2304]{3,2,1,0:T(8,128)(2,1)}, u32[]{:S(2)}) copy-start(bf16[1,2,64,2304]{3,2,1,0:T(8,128)(2,1)} %param.23) | copy-start | bytes 1769476
  6.5 59.7 %all-gather.2.cloned.1.call-start = ((), (), s32[]{:S(2)}) async-start(), calls=%async_computation.2 | async-start | bytes 1327104 | tf_op jit(solution)/shard_map/all_gather | solution.py:58
  18.9 17.9 %copy-start.8 = (s32[1,2]{1,0:T(1,128)S(1)}, s32[1,2]{1,0:T(1,128)}, u32[]{:S(2)}) copy-start(s32[1,2]{1,0:T(1,128)} %param.20) | copy-start | bytes 28
  19.4 17.5 %copy-start.4 = (bf16[2,16,2304]{2,1,0:T(8,128)(2,1)S(1)}, bf16[2,16,2304]{2,1,0:T(8,128)(2,1)}, u32[]{:S(2)}) copy-start(bf16[2,16,2304]{2,1,0:T(8,128)(2,1)} %param.16) | copy-start | bytes 442372
  20.2 1050.6 %all-reduce.3.cloned.1.call-start = ((), (), s32[]{:S(2)}) async-start(), calls=%async_computation.3 | async-start | bytes 4718592 | tf_op jit(solution)/shard_map/psum | solution.py:108
  69.6 494.6 %copy-start.1 = (bf16[1,2,64,2304]{2,3,1,0:T(8,128)(2,1)S(1)}, bf16[1,2,64,2304]{2,3,1,0:T(8,128)(2,1)}, u32[]{:S(2)}) copy-start(bf16[1,2,64,2304]{2,3,1,0:T(8,128)(2,1)} %copy.110) | copy-start | bytes 1769476
  574.7 0.8 copy-start.5
  574.7 652.8 %all-reduce.5.cloned.1.call-start = ((), (), s32[]{:S(2)}) async-start(), calls=%async_computation.4 | async-start | bytes 884736 | tf_op jit(solution)/shard_map/psum | solution.py:150
  1070.7 27.2 %copy-start.6 = (f32[2304]{0:T(1024)S(1)}, f32[2304]{0:T(1024)}, u32[]{:S(2)}) copy-start(f32[2304]{0:T(1024)} %param.24) | copy-start | bytes 27652
  1118.7 2.8 copy-start.2
  1121.3 115.0 %copy-start.7 = (bf16[2,16,2]{1,2,0:T(2,128)(2,1)S(1)}, bf16[2,16,2]{1,2,0:T(2,128)(2,1)}, u32[]{:S(2)}) copy-start(bf16[2,16,2]{1,2,0:T(2,128)(2,1)} %param.18) | copy-start | bytes 388
  1229.6 22.9 %all-to-all-start.1 = ((bf16[8,2,6,2304]{3,1,2,0:T(2,128)(2,1)}), bf16[8,2,6,2304]{3,1,2,0:T(2,128)(2,1)S(1)}, u32[]{:S(2)}, u32[]{:S(2)}) async-start(bf16[8,2,6,2304]{3,1,2,0:T(2,128)(2,1)} %copy.105), calls=%async_computation.1 | async-start | bytes 884736 | tf_op jit(solution)/shard_map/all_to_all | solution.py:151
Sparse Core Ops, SparseCore 0:
  20.3 45.9 all-gather.1
  574.8 197.8 all-reduce.2
  1122.6 104.7 all-reduce.4
where the time goes:
time: 1260 us
  blocking collectives  1060 us (84%)
  waiting for transfers between devices  131 us (10%)
  local copies, waits for them, and re-layouts  20.2 us (2%)
  between operations  13.4 us (1%)
  matrix products  12.9 us (1%)
    psum x1, blocking collectives, on_device(): context_all, totals_all = lax.psum((context, totals), ('exp', 'shard'))  491 us
    pmax x1, blocking collectives, on_device(): row_peak = lax.pmax(local_peak, ('exp', 'shard'))  490 us
    psum x1, waiting for transfers between devices, on_device(): expert_out = lax.psum(partial_out.astype(jnp.bfloat16), 'shard')  105 us
  transfers between devices with their start and end apart: 4, of which 3 were waited for; matrix products, arithmetic and copies ran while one was open for 1% of the time, Pallas kernels for 0%

commit v1 on v0

--- a/solution.py
+++ b/solution.py
@@ -3,6 +3,7 @@
 import jax.numpy as jnp
 from jax import lax
 from jax.sharding import PartitionSpec as P
+from jax.lax import all_gather
 
 H = 36
 NEG_FILL = -1e30
@@ -147,7 +148,8 @@
         gate_up,
         down_proj,
     )
-    expert_out = lax.psum(partial_out.astype(jnp.bfloat16), "shard")
+    figure_lay = lambda piece_in: all_gather(piece_in, "shard").sum(axis=0)
+    expert_out = figure_lay(partial_out.astype(jnp.bfloat16))
     returned = lax.all_to_all(expert_out, "exp", split_axis=0, concat_axis=0, tiled=True)
     moe_term = jnp.einsum(
         "jtnc,njcd->jtd", share_table, returned, preferred_element_type=jnp.float32

time: 1260 us -> 1200 us (0.952)
  waiting for transfers between devices: 131 us -> 70 us
    psum x1 -> x0, waiting for transfers between devices: 105 us -> none  [on_device(): expert_out = lax.psum(partial_out.astype(jnp.bfloat16), 'shard')]
    all_gather x0 -> x1, waiting for transfers between devices: none -> 44.2 us  [on_device(): figure_lay = lambda piece_in: all_gather(piece_in, 'shard').sum(axis=0)]
where the time goes in v1:
time: 1200 us
  blocking collectives  1060 us (88%)
  waiting for transfers between devices  70 us (6%)
  local copies, waits for them, and re-layouts  18.9 us (2%)
  other arithmetic  15.8 us (1%)
  between operations  13.4 us (1%)
  matrix products  13.1 us (1%)
    psum x1, blocking collectives, on_device(): context_all, totals_all = lax.psum((context, totals), ('exp', 'shard'))  491 us
    pmax x1, blocking collectives, on_device(): row_peak = lax.pmax(local_peak, ('exp', 'shard'))  490 us
    all_gather x1, waiting for transfers between devices, on_device(): figure_lay = lambda piece_in: all_gather(piece_in, 'shard').sum(axis=0)  44.2 us
  transfers between devices with their start and end apart: 4, of which 3 were waited for; matrix products, arithmetic and copies ran while one was open for 1% of the time, Pallas kernels for 0%

profile of v1, /device:TPU:1, one launch (start us, length us, event | category | flops | bytes accessed | tf_op | source)
XLA Modules:
  0.0 1202.0 jit_solution(11537990163666701545)
XLA Ops:
  6.5 0.9 compare_and_fusion
  7.4 11.4 all_gather.25
  18.9 0.6 gather_fusion.5
  19.4 0.7 broadcast_select_fusion
  20.3 0.7 add_bitcast_fusion
  20.9 0.2 reduce-window.4
  21.1 0.7 fusion.29
  21.8 8.4 all_gather.28
  30.2 0.6 gather_fusion.2
  31.1 0.9 fusion.26
  32.0 0.2 fusion.27
  32.2 2.3 copy.111
  34.5 2.0 reshape_squeeze.6
  36.5 0.2 select_reduce_fusion.5
  36.7 11.1 all_gather.24
  48.2 18.2 %all-gather.4.cloned.1.call-done = bf16[2,128,2304]{2,1,0:T(8,128)(2,1)} async-done(((bf16[2,16,2304]{2,1,0:T(8,128)(2,1)}), bf16[2,128,2304]{2,1,0:T(8,128)(2,1)}) %all-gather.4.cloned.1.call-update) | async-done | bytes 1179664 | tf_op jit(solution)/shard_map/all_gather | solution.py:59
  66.3 1.9 gather_fusion
  68.2 1.4 copy.91
  69.7 3.9 fusion.3
  73.6 490.0 %pmax.7 = f32[2,36,128]{2,1,0:T(8,128)S(1)} all-reduce(f32[2,36,128]{2,1,0:T(8,128)S(1)} %copy.93), channel_id=1, replica_groups=mesh['req'=4,'exp'=8,'shard'=16] {'exp','shard'}, use_global_device_ids=true, to_apply=%region_7.9 | all-reduce | flops 9216 | bytes 73728 | tf_op jit(solution)/shard_map/pmax | solution.py:97
  563.6 0.5 gather_fusion.1
  564.3 3.7 fusion.32
  567.9 3.1 copy.95
  571.0 3.7 select_reduce_fusion
  574.8 0.2 select_reduce_fusion.3
  575.2 1.6 gather_fusion.4
  576.9 2.4 convert_reduce_fusion
  579.4 491.2 %psum.15 = f32[2,36,128]{2,0,1:T(2,128)S(1)} all-reduce(f32[2,36,128]{2,0,1:T(2,128)S(1)} %select_reduce_fusion.1), channel_id=1, replica_groups=mesh['req'=4,'exp'=8,'shard'=16] {'exp','shard'}, use_global_device_ids=true, to_apply=%region_12.14 | all-reduce | flops 9216 | bytes 73728 | tf_op jit(solution)/shard_map/psum | solution.py:109
  1070.8 0.2 div.23
  1071.0 0.2 div.24
  1071.2 1.5 convolution_convert_fusion.2
  1072.7 0.2 copy.97
  1072.9 23.8 %all_gather.27 = bf16[2,16,2304]{1,0,2:T(2,128)(2,1)S(1)} all-gather(bf16[2,16,144]{1,0,2:T(2,128)(2,1)S(1)} %copy.97), channel_id=1, replica_groups=mesh['req'=4,'exp'=8,'shard'=16] {'shard'}, dimensions={2}, use_global_device_ids=true | all-gather | bytes 156672 | tf_op jit(solution)/shard_map/all_gather | solution.py:121
  1096.7 1.4 copy.98
  1098.1 0.2 multiply_reduce_fusion
  1098.4 0.3 fusion
  1098.7 0.3 copy.101
  1099.1 19.8 %all_to_all.10 = bf16[8,2,6,2304]{3,1,2,0:T(2,128)(2,1)S(1)} all-to-all(bf16[8,2,6,2304]{3,1,2,0:T(2,128)(2,1)S(1)} %copy.101), channel_id=1, replica_groups=mesh['req'=4,'exp'=8,'shard'=16] {'exp'}, dimensions={0} | all-to-all | bytes 884736 | tf_op jit(solution)/shard_map/all_to_all | solution.py:147
  1119.0 0.6 fusion.4
  1119.8 2.2 convolution_convert_fusion.1
  1122.1 44.2 %all-gather.6.cloned.1.call-done = bf16[128,2,6,2304]{3,0,2,1:T(8,128)(2,1)} async-done(((bf16[8,2,6,2304]{3,0,2,1:T(8,128)(2,1)}), bf16[128,2,6,2304]{3,0,2,1:T(8,128)(2,1)}) %all-gather.6.cloned.1.call-update) | async-done | bytes 7077904 | tf_op jit(solution)/shard_map/all_gather | solution.py:151
  1166.3 3.9 bitcast_reduce_fusion
  1170.2 1.1 copy.106
  1171.3 7.1 all-to-all-start.1
  1178.4 7.9 all_gather.29
  1186.3 0.6 gather_fusion.3
  1187.0 7.6 all-to-all-done.1
  1194.6 0.9 fusion.2
  (56 shorter events, 2.1 us)
Async XLA Ops:
  6.5 1112.5 %copy-start = (bf16[1,2,180,2304]{3,1,2,0:T(2,128)(2,1)S(1)}, bf16[1,2,180,2304]{3,1,2,0:T(2,128)(2,1)}, u32[]{:S(2)}) copy-start(bf16[1,2,180,2304]{3,1,2,0:T(2,128)(2,1)} %param.26) | copy-start | bytes 4976644
  6.5 28.0 %copy-start.2 = (bf16[1,2,64,2304]{3,2,1,0:T(8,128)(2,1)S(1)}, bf16[1,2,64,2304]{3,2,1,0:T(8,128)(2,1)}, u32[]{:S(2)}) copy-start(bf16[1,2,64,2304]{3,2,1,0:T(8,128)(2,1)} %param.22) | copy-start | bytes 1769476
  6.5 59.8 %all-gather.4.cloned.1.call-start = ((), (), s32[]{:S(2)}) async-start(), calls=%async_computation.2 | async-start | bytes 1327104 | tf_op jit(solution)/shard_map/all_gather | solution.py:59
  18.9 17.7 %copy-start.6 = (s32[1,2]{1,0:T(1,128)S(1)}, s32[1,2]{1,0:T(1,128)}, u32[]{:S(2)}) copy-start(s32[1,2]{1,0:T(1,128)} %param.20) | copy-start | bytes 28
  18.9 17.8 %copy-start.3 = (bf16[2,16,2304]{2,1,0:T(8,128)(2,1)S(1)}, bf16[2,16,2304]{2,1,0:T(8,128)(2,1)}, u32[]{:S(2)}) copy-start(bf16[2,16,2304]{2,1,0:T(8,128)(2,1)} %param.16) | copy-start | bytes 442372
  20.2 1051.0 %all-reduce.2.cloned.1.call-start = ((), (), s32[]{:S(2)}) async-start(), calls=%async_computation.3 | async-start | bytes 4718592 | tf_op jit(solution)/shard_map/psum | solution.py:109
  69.7 494.6 %copy-start.1 = (bf16[1,2,64,2304]{2,3,1,0:T(8,128)(2,1)S(1)}, bf16[1,2,64,2304]{2,3,1,0:T(8,128)(2,1)}, u32[]{:S(2)}) copy-start(bf16[1,2,64,2304]{2,3,1,0:T(8,128)(2,1)} %copy.111) | copy-start | bytes 1769476
  574.8 591.5 %all-gather.6.cloned.1.call-start = ((), (), s32[]{:S(2)}) async-start(), calls=%async_computation.4 | async-start | bytes 7520256 | tf_op jit(solution)/shard_map/all_gather | solution.py:151
  1071.2 27.2 %copy-start.4 = (f32[2304]{0:T(1024)S(1)}, f32[2304]{0:T(1024)}, u32[]{:S(2)}) copy-start(f32[2304]{0:T(1024)} %param.24) | copy-start | bytes 27652
  1122.1 56.3 %copy-start.5 = (bf16[2,16,2]{1,2,0:T(2,128)(2,1)S(1)}, bf16[2,16,2]{1,2,0:T(2,128)(2,1)}, u32[]{:S(2)}) copy-start(bf16[2,16,2]{1,2,0:T(2,128)(2,1)} %param.18) | copy-start | bytes 388
  1171.3 23.3 %all-to-all-start.1 = ((bf16[8,2,6,2304]{3,1,2,0:T(2,128)(2,1)}), bf16[8,2,6,2304]{3,1,2,0:T(2,128)(2,1)S(1)}, u32[]{:S(2)}, u32[]{:S(2)}) async-start(bf16[8,2,6,2304]{3,1,2,0:T(2,128)(2,1)} %copy.106), calls=%async_computation.1 | async-start | bytes 884736 | tf_op jit(solution)/shard_map/all_to_all | solution.py:153
Sparse Core Ops, SparseCore 0:
  20.3 45.9 all-gather.3
  574.9 197.8 all-reduce.1
  1122.2 44.0 all-gather.5
